TPU v7x, 512 devices: a whole 4x4x16 slice. The times are simulated.
512 devices in a mesh: dp: 32 (over z, core), expert: 16 (over x, y).
Axes of the slice: x: 4, y: 4, z: 16, core: 2. Of those that a mesh axis runs over, the one named last changes fastest.
Arguments:
- grad_out: bfloat16 [65536, 2048], P(('dp', 'expert')), may hold values from -6 to 6
- gate: float32 [65536, 1], P(('dp', 'expert')), may hold values from 0.25 to 1
- expert_ids: int32 [65536, 1], P(('dp', 'expert')), may hold values from 0 to 15; in each aligned block of 128 rows (0 to 127, 128 to 255, ...) at most 10 rows name the same one
- w_in: bfloat16 [16, 5120, 2048], P('expert', 'dp'), may hold values from -0.125 to 0.125
- w_out: bfloat16 [16, 5120, 2048], P('expert', 'dp'), may hold values from -0.078125 to 0.078125
- pre_act: bfloat16 [32, 16, 160, 5120], P('dp', 'expert'), may hold values from -6 to 6
Outputs:
- grad_in: bfloat16 [65536, 2048], P(('dp', 'expert'))
Inputs may be any that keep to these rules, and one draw needn't show every extreme that they name: `expert_ids`: among the 128 tokens of one device no expert is named more than 10 times, and in every draw some device names some expert exactly 10 times.
All inputs are finite; a program needn't handle non-finite values.
Results may differ from a plain program's by a relative error of at most 0.0057.
Values may be sent and summed in bfloat16 or wider, within the bound.
No kernel may reach another device: no remote copies, remote signals or barrier semaphores. Data moves between devices by JAX's collectives and lax.ppermute only.
A program may use at most 192 MiB of HBM per device.

v0:
```python
import jax
import jax.numpy as jnp
from jax import lax
from jax.sharding import PartitionSpec as P


def gelu_slope(values):
    inside = 0.7978845608028654 * (values + 0.044715 * values * values * values)
    curved = jnp.tanh(inside)
    return 0.5 * (1.0 + curved) + 0.5 * values * (1.0 - curved * curved) * 0.7978845608028654 * (
        1.0 + 3.0 * 0.044715 * values * values
    )


def body(grad_out, gate, expert_ids, w_in, w_out, pre_act):
    groups = lax.axis_size("expert")
    slots = pre_act.shape[2]
    capacity = slots // groups
    width = grad_out.shape[1]
    chosen = expert_ids[:, 0]
    hit_table = (chosen[:, None] == jnp.arange(groups, dtype=jnp.int32)[None, :]).astype(jnp.int32)
    position = jnp.sum(jnp.cumsum(hit_table, axis=0) * hit_table, axis=1) - 1
    target = chosen * capacity + position
    scaled = (grad_out.astype(jnp.float32) * gate).astype(jnp.bfloat16)
    outgoing = (
        jnp.zeros((slots, width), jnp.bfloat16)
        .at[target]
        .set(scaled)
        .reshape(groups, capacity, width)
    )
    arrived = lax.all_to_all(outgoing, "expert", split_axis=0, concat_axis=0, tiled=True)
    rows_in = arrived.reshape(slots, width)
    stashed = pre_act[0, 0]
    shards = lax.axis_size("dp")
    rows = w_out.shape[1]
    both = jnp.concatenate([w_out, w_in], axis=1)
    gathered = lax.all_gather(both, "dp", axis=1, tiled=True).reshape(shards, 2, rows, width)
    hidden_grad = jnp.einsum(
        "sd,gfd->sgf", rows_in, gathered[:, 0], preferred_element_type=jnp.float32
    ).reshape(slots, shards * rows)
    act_grad = (hidden_grad * gelu_slope(stashed.astype(jnp.float32))).astype(jnp.bfloat16)
    slot_sum = jnp.einsum(
        "sgf,gfd->sd",
        act_grad.reshape(slots, shards, rows),
        gathered[:, 1],
        preferred_element_type=jnp.float32,
    )
    slot_grad = slot_sum.astype(jnp.bfloat16).reshape(groups, capacity, width)
    returned = lax.all_to_all(slot_grad, "expert", split_axis=0, concat_axis=0, tiled=True)
    return returned.reshape(slots, width)[target]


def solution(mesh):
    return jax.shard_map(
        body,
        mesh=mesh,
        in_specs=(
            P(("dp", "expert"), None),
            P(("dp", "expert"), None),
            P(("dp", "expert"), None),
            P("expert", "dp", None),
            P("expert", "dp", None),
            P("dp", "expert", None, None),
        ),
        out_specs=P(("dp", "expert"), None),
        check_vma=False,
    )
```

profile of v0, /device:TPU:8, one launch (start us, length us, event | category | flops | bytes accessed | tf_op | source)
XLA Modules:
  0.0 328.3 jit_solution(9330431443200145467)
XLA Ops:
  6.5 0.0 copy-start.1
  6.5 0.0 copy-start.2
  6.5 0.0 copy-start
  6.5 0.0 all-gather.2.cloned.1.call-start
  6.5 2.5 pad_maximum_fusion
  9.1 0.0 all-gather.2.cloned.1.call-update
  9.1 0.0 copy-done.1
  9.1 0.1 fusion.19
  9.2 0.2 reduce_window_sum.11
  9.4 0.2 select_reduce_fusion
  9.6 0.0 copy-done.2
  9.6 0.0 copy-done
  9.6 1.6 scatter_custom_fusion
  11.2 0.2 reshape.32
  11.4 22.9 %all_to_all.10 = bf16[16,10,2048]{2,1,0:T(8,128)(2,1)S(1)} all-to-all(bf16[16,10,2048]{2,1,0:T(8,128)(2,1)S(1)} %reshape.32), channel_id=1, replica_groups=mesh['dp'=32,'expert'=16] {'expert'}, dimensions={0} | all-to-all | bytes 1310720 | tf_op jit(solution)/shard_map/all_to_all | solution.py:31
  34.4 0.2 reshape.33
  34.6 212.7 %all-gather.2.cloned.1.call-done = bf16[1,10240,2048]{2,1,0:T(8,128)(2,1)} async-done(((bf16[1,320,2048]{2,1,0:T(8,128)(2,1)}), bf16[1,10240,2048]{2,1,0:T(8,128)(2,1)}) %all-gather.2.cloned.1.call-update) | async-done | bytes 41943056 | tf_op jit(solution)/shard_map/all_gather | solution.py:37
  247.3 0.0 copy-start.3
  247.3 17.8 %slice.10 = bf16[32,1,160,2048]{3,2,1,0:T(8,128)(2,1)} slice(bf16[32,2,160,2048]{3,2,1,0:T(8,128)(2,1)} %bitcast.29), slice={[0:32], [0:1], [0:160], [0:2048]} | slice | bytes 41943040 | tf_op jit(solution)/shard_map/slice | solution.py:39
  265.0 0.0 copy-done.3
  265.0 13.3 %fusion.1 = bf16[160,5120]{1,0:T(8,128)(2,1)} fusion(bf16[160,2048]{1,0:T(8,128)(2,1)S(1)} %reshape.33, bf16[5120,2048]{1,0:T(8,128)(2,1)} %bitcast.28, bf16[1,1,160,5120]{3,2,1,0:T(8,128)(2,1)S(1)} %copy-done.3), kind=kOutput, calls=%fused_computation.12 | convolution fusion | flops 3371827200 | bytes 24903680 | tf_op jit(solution)/shard_map/sd,gfd->sgf/dot_general | solution.py:38
  278.3 4.4 %reshape.35 = bf16[160,32,160]{2,1,0:T(8,128)(2,1)S(1)} reshape(bf16[160,5120]{1,0:T(8,128)(2,1)} %fusion.1) | data formatting | bytes 3276800 | tf_op jit(solution)/shard_map/reshape | solution.py:44
  282.8 11.4 %fusion.13 = bf16[160,2048]{1,0:T(8,128)(2,1)S(1)} fusion(bf16[32,2,160,2048]{3,2,1,0:T(8,128)(2,1)} %bitcast.30, bf16[160,32,160]{2,1,0:T(8,128)(2,1)S(1)} %reshape.35), kind=kOutput, calls=%fused_computation.22 | convolution fusion | flops 3355770880 | bytes 23265280 | tf_op jit(solution)/shard_map/sgf,gfd->sd/dot_general | solution.py:42
  294.2 1.2 reshape.36
  295.4 7.3 %all-to-all-start.1 = ((bf16[16,10,2048]{2,1,0:T(8,128)(2,1)}), bf16[16,10,2048]{2,1,0:T(8,128)(2,1)S(1)}, u32[]{:S(2)}, u32[]{:S(2)}) async-start(bf16[16,10,2048]{2,1,0:T(8,128)(2,1)} %reshape.36), calls=%async_computation.1 | async-start | bytes 2097152 | tf_op jit(solution)/shard_map/all_to_all | solution.py:49
  302.7 16.8 %all-to-all-done.1 = bf16[16,10,2048]{2,1,0:T(8,128)(2,1)S(1)} async-done(((bf16[16,10,2048]{2,1,0:T(8,128)(2,1)}), bf16[16,10,2048]{2,1,0:T(8,128)(2,1)S(1)}, u32[]{:S(2)}, u32[]{:S(2)}) %all-to-all-start.1) | async-done | bytes 655392 | tf_op jit(solution)/shard_map/all_to_all | solution.py:49
  319.5 0.2 reshape.37
  319.8 1.7 gather_fusion
  (2 shorter events, 0.0 us)
Async XLA Ops:
  6.5 2.6 copy-start.1
  6.5 3.0 copy-start.2
  6.5 3.1 copy-start
  6.5 240.7 %all-gather.2.cloned.1.call-start = ((), (), s32[]{:S(2)}) async-start(), calls=%async_computation.2 | async-start | bytes 43253760 | tf_op jit(solution)/shard_map/all_gather | solution.py:37
  247.3 17.8 %copy-start.3 = (bf16[1,1,160,5120]{3,2,1,0:T(8,128)(2,1)S(1)}, bf16[1,1,160,5120]{3,2,1,0:T(8,128)(2,1)}, u32[]{:S(2)}) copy-start(bf16[1,1,160,5120]{3,2,1,0:T(8,128)(2,1)} %param.11) | copy-start | bytes 4915204
  295.4 24.1 %all-to-all-start.1 = ((bf16[16,10,2048]{2,1,0:T(8,128)(2,1)}), bf16[16,10,2048]{2,1,0:T(8,128)(2,1)S(1)}, u32[]{:S(2)}, u32[]{:S(2)}) async-start(bf16[16,10,2048]{2,1,0:T(8,128)(2,1)} %reshape.36), calls=%async_computation.1 | async-start | bytes 2097152 | tf_op jit(solution)/shard_map/all_to_all | solution.py:49
Sparse Core Ops, SparseCore 0:
  9.5 237.7 all-gather.1
where the time goes:
time: 329 us; the launch traced here: 328 us
  waiting for transfers between devices  230 us (70%)
  local copies, waits for them, and re-layouts  25.8 us (8%)
  matrix products  24.7 us (8%)
  blocking collectives  22.9 us (7%)
  between operations  13.5 us (4%)
  starting transfers between devices  7.26 us (2%)
  other arithmetic  4.6 us (1%)
    all_gather x1, waiting for transfers between devices, body(): lax.all_gather(both, 'dp', axis=1, tiled=True)  213 us
    all_to_all x1, blocking collectives, body(): lax.all_to_all(outgoing, 'expert', split_axis=0, concat_axis=0, tiled=True)  22.9 us
    slice x1, local copies, waits for them, and re-layouts, body(): gathered[:, 0]  17.8 us
    all_to_all x1, waiting for transfers between devices, body(): lax.all_to_all(slot_grad, 'expert', split_axis=0, concat_axis=0, tiled=True)  16.8 us
    dot_general x1, matrix products, body(): jnp.einsum('sd,gfd->sgf', rows_in, gathered[:, 0], preferred_element_type...  13.3 us
    dot_general x1, matrix products, body(): jnp.einsum('sgf,gfd->sd', act_grad.reshape(slots, shards, rows), gathered...  11.4 us
    all_to_all x1, starting transfers between devices, body(): lax.all_to_all(slot_grad, 'expert', split_axis=0, concat_axis=0, tiled=True)  7.26 us
  transfers between devices with their start and end apart: 2, of which 2 were waited for; matrix products, arithmetic and copies ran while one was open for 1% of the time, Pallas kernels for 0%

commit v1 on v0

--- a/solution.py
+++ b/solution.py
@@ -2,6 +2,11 @@
 import jax.numpy as jnp
 from jax import lax
 from jax.sharding import PartitionSpec as P
+
+
+def gather_from_all(x, axis, dim):
+    copies = jnp.concatenate([x] * lax.axis_size(axis), axis=dim)
+    return lax.all_to_all(copies, axis, dim, dim, tiled=True)
 
 
 def gelu_slope(values):
@@ -34,7 +39,7 @@
     shards = lax.axis_size("dp")
     rows = w_out.shape[1]
     both = jnp.concatenate([w_out, w_in], axis=1)
-    gathered = lax.all_gather(both, "dp", axis=1, tiled=True).reshape(shards, 2, rows, width)
+    gathered = gather_from_all(both, "dp", 1).reshape(shards, 2, rows, width)
     hidden_grad = jnp.einsum(
         "sd,gfd->sgf", rows_in, gathered[:, 0], preferred_element_type=jnp.float32
     ).reshape(slots, shards * rows)

time: 329 us -> 2500 us (7.60)
  the two profiles are of different devices: /device:TPU:8 before, /device:TPU:32 now
where the time goes in v1:
time: 2500 us; the launch traced here: 2490 us
  waiting for transfers between devices  1820 us (73%)
  local copies, waits for them, and re-layouts  360 us (14%)
  other arithmetic  249 us (10%)
  starting transfers between devices  30 us (1%)
  matrix products  26.4 us (1%)
    all_to_all x1, waiting for transfers between devices, gather_from_all(): return lax.all_to_all(copies, axis, dim, dim, tiled=True)  1810 us
    unnamed x75, local copies, waits for them, and re-layouts  331 us
    unnamed x1, other arithmetic  244 us
  transfers between devices with their start and end apart: 3, of which 2 were waited for; matrix products, arithmetic and copies ran while one was open for 19% of the time, Pallas kernels for 0%

profile of v1, /device:TPU:32, one launch (start us, length us, event | category | flops | bytes accessed | tf_op | source)
XLA Modules:
  0.0 2489.6 jit_solution(2414546131878348559)
XLA Ops:
  5.8 7.0 all-to-all-start
  12.9 3.2 constant_dynamic-update-slice_fusion.63
  16.1 3.2 constant_dynamic-update-slice_fusion.62
  19.2 3.2 constant_dynamic-update-slice_fusion.61
  22.4 3.2 constant_dynamic-update-slice_fusion.60
  25.6 3.2 constant_dynamic-update-slice_fusion.59
  28.8 3.2 constant_dynamic-update-slice_fusion.58
  32.0 3.3 constant_dynamic-update-slice_fusion.57
  35.2 3.2 constant_dynamic-update-slice_fusion.56
  38.4 3.2 constant_dynamic-update-slice_fusion.55
  41.5 3.2 constant_dynamic-update-slice_fusion.54
  44.8 3.2 constant_dynamic-update-slice_fusion.53
  47.9 3.5 constant_dynamic-update-slice_fusion.52
  51.4 3.2 constant_dynamic-update-slice_fusion.51
  54.6 3.2 constant_dynamic-update-slice_fusion.50
  57.7 3.2 constant_dynamic-update-slice_fusion.49
  60.9 3.2 constant_dynamic-update-slice_fusion.48
  64.1 3.2 constant_dynamic-update-slice_fusion.47
  67.2 3.2 constant_dynamic-update-slice_fusion.46
  70.4 3.2 constant_dynamic-update-slice_fusion.45
  73.6 3.2 constant_dynamic-update-slice_fusion.44
  80.0 3.2 constant_dynamic-update-slice_fusion.42
  83.1 3.4 constant_dynamic-update-slice_fusion.41
  86.5 3.2 constant_dynamic-update-slice_fusion.40
  89.7 3.2 constant_dynamic-update-slice_fusion.39
  92.8 3.2 constant_dynamic-update-slice_fusion.38
  96.0 3.2 constant_dynamic-update-slice_fusion.37
  102.3 3.2 constant_dynamic-update-slice_fusion.35
  105.5 3.2 constant_dynamic-update-slice_fusion.34
  108.7 3.2 constant_dynamic-update-slice_fusion.33
  115.0 3.2 constant_dynamic-update-slice_fusion.31
  118.2 3.4 constant_dynamic-update-slice_fusion.30
  124.8 3.2 constant_dynamic-update-slice_fusion.28
  127.9 3.2 constant_dynamic-update-slice_fusion.27
  134.3 3.2 constant_dynamic-update-slice_fusion.25
  137.5 3.2 constant_dynamic-update-slice_fusion.24
  191.9 244.4 %reduce = bf16[10240,2048]{1,0:T(8,128)(2,1)} reduce(bf16[10240,1,2048]{2,1,0:T(2,128)(2,1)} %bitcast.26, bf16[]{:T(256)} %broadcast.51), dimensions={1}, to_apply=%bitcast.26.reduce_sub_computation | reduce | bytes 83886080
  436.3 46.7 %reshape.58 = bf16[32,2,327680]{2,1,0:T(2,128)(2,1)} reshape(bf16[10240,2048]{1,0:T(8,128)(2,1)} %reduce) | data formatting | bytes 83886080
  483.0 15.8 all-to-all-start.1
  499.0 1806.9 %all-to-all-done.1 = bf16[32,2,327680]{2,1,0:T(2,128)(2,1)} async-done(((bf16[32,2,327680]{2,1,0:T(2,128)(2,1)}), bf16[32,2,327680]{2,1,0:T(2,128)(2,1)}, u32[]{:S(2)}, u32[]{:S(2)}) %all-to-all-start.1) | async-done | bytes 41943072 | tf_op jit(solution)/shard_map/all_to_all | solution.py:9
  2305.9 57.2 %reshape.59 = bf16[10240,1,2048]{2,1,0:T(2,128)(2,1)} reshape(bf16[32,2,327680]{2,1,0:T(2,128)(2,1)} %all-to-all-done.1) | data formatting | bytes 83886080
  2363.1 50.6 %copy.76 = bf16[1,10240,2048]{2,1,0:T(8,128)(2,1)} copy(bf16[1,10240,2048]{2,0,1:T(2,128)(2,1)} %bitcast.27) | data formatting | bytes 83886080
  2413.7 17.6 slice.10
  2431.3 12.5 fusion.1
  2443.9 4.2 reshape.35
  2448.1 13.9 fusion.13
  2463.1 7.2 all-to-all-start.2
  2470.4 16.8 all-to-all-done.2
  (50 shorter events, 76.2 us)
Async XLA Ops:
  0.0 140.7 %copy-start = (bf16[1,160,2048]{2,1,0:T(8,128)(2,1)S(1)}, bf16[1,160,2048]{2,1,0:T(8,128)(2,1)}, u32[]{:S(2)}) copy-start(bf16[1,160,2048]{2,1,0:T(8,128)(2,1)} %param.10) | copy-start | bytes 1966084
  0.0 142.7 %copy-start.1 = (bf16[1,160,2048]{2,1,0:T(8,128)(2,1)S(1)}, bf16[1,160,2048]{2,1,0:T(8,128)(2,1)}, u32[]{:S(2)}) copy-start(bf16[1,160,2048]{2,1,0:T(8,128)(2,1)} %param.9) | copy-start | bytes 1966084
  2.5 3.3 copy-start.2
  5.8 477.1 %all-to-all-start = ((bf16[16,10,2048]{2,1,0:T(8,128)(2,1)}), bf16[16,10,2048]{2,1,0:T(8,128)(2,1)S(1)}, u32[]{:S(2)}, u32[]{:S(2)}) async-start(bf16[16,10,2048]{2,1,0:T(8,128)(2,1)} %reshape.32), calls=%async_computation | async-start | bytes 2097152 | tf_op jit(solution)/shard_map/all_to_all | solution.py:36
  483.0 1822.9 %all-to-all-start.1 = ((bf16[32,2,327680]{2,1,0:T(2,128)(2,1)}), bf16[32,2,327680]{2,1,0:T(2,128)(2,1)}, u32[]{:S(2)}, u32[]{:S(2)}) async-start(bf16[32,2,327680]{2,1,0:T(2,128)(2,1)} %reshape.58), calls=%async_computation.1 | async-start | bytes 83886080 | tf_op jit(solution)/shard_map/all_to_all | solution.py:9
  2413.7 56.6 %copy-start.3 = (s32[128]{0:T(128)S(1)}, s32[128]{0:T(128)}, u32[]{:S(2)}) copy-start(s32[128]{0:T(128)} %copy-done.2) | copy-start | bytes 1540
  2463.1 24.1 all-to-all-start.2
